TPU v7x, 256 devices: a whole 4x4x8 slice. The times are simulated.
256 devices in a mesh: tile: 16 (over y, x), query: 2 (over core), dp: 8 (over z).
Axes of the slice: x: 4, y: 4, z: 8, core: 2. Of those that a mesh axis runs over, the one named last changes fastest.
Arguments:
- features: bfloat16 [8, 131072, 256], P('dp', ('tile', 'query')), may hold values from -6 to 6
- queries: bfloat16 [8, 256, 256], P('dp', ('tile', 'query')), may hold values from -6 to 6
- out_grad: bfloat16 [8, 256, 256], P('dp', ('tile', 'query')), may hold values from -48 to 48
- value_weight: bfloat16 [256, 256], replicated, may hold values from -0.375 to 0.375
- attn_weight: bfloat16 [256, 128], replicated, may hold values from -0.375 to 0.375
- out_weight: bfloat16 [256, 256], replicated, may hold values from -0.375 to 0.375
- slot_point: int32 [8, 65536], P('dp', ('tile', 'query')), may hold values from 0 to 32767, as said below
- slot_rows: int32 [8, 4, 65536], P('dp', None, ('tile', 'query')), may hold values from 0 to 4095, as said below
- slot_bilinear: float32 [8, 4, 65536], P('dp', None, ('tile', 'query')), may hold values from 0 to 1, as said below
- slot_count: int32 [8, 32], P('dp', ('tile', 'query')), may hold values from 1 to 2048, as said below
Outputs:
- feature_grad: bfloat16 [8, 131072, 256], P('dp', ('tile', 'query'))
- query_grad: bfloat16 [8, 256, 256], P('dp', ('tile', 'query'))
- value_weight_grad: float32 [256, 256], replicated
- attn_weight_grad: float32 [256, 128], replicated
- out_weight_grad: float32 [256, 256], replicated
Inputs may be any that keep to these rules, and one draw needn't show every extreme that they name: `slot_count`: per page one owner has exactly 2048 live slots; the counts of a page sum to 32768. `slot_point`: the live slots of a page name every sample point exactly once, point m = q * 128 + head * 4 * 4 + level * 4 + point; slots that are not live hold arbitrary point numbers. `slot_rows`: the corners of a slot are rows r, r + 1, r + 64, r + 65 of the owner's tokens laid out in lines of 64. `slot_bilinear`: the four weights of a slot sum to one.
All inputs are finite; a program needn't handle non-finite values.
Results may differ from a plain program's by a relative error of at most 0.0064.
Values may be sent and summed in bfloat16 or wider, within the bound.
No kernel may reach another device: no remote copies, remote signals or barrier semaphores. Data moves between devices by JAX's collectives and lax.ppermute only.
A program may use at most 128 MiB of HBM per device.

v0:
```python
import jax
import jax.numpy as jnp
from jax import lax
from jax.sharding import PartitionSpec as P

HEADS = 8
TILE_W = 64


def over_rows(left, right):
    return lax.dot_general(
        left, right, (((0,), (0,)), ((), ())), preferred_element_type=jnp.float32
    )


def over_rows_exact(left, right):
    return lax.dot_general(
        left,
        right,
        (((0,), (0,)), ((), ())),
        precision=lax.Precision.HIGHEST,
        preferred_element_type=jnp.float32,
    )


def times_transpose(left, right):
    return lax.dot_general(
        left, right, (((1,), (1,)), ((), ())), preferred_element_type=jnp.float32
    )


def shift_down(block, offset):
    return jnp.concatenate(
        [jnp.zeros((offset, block.shape[1]), block.dtype), block[: block.shape[0] - offset]], axis=0
    )


def local(
    features,
    queries,
    out_grad,
    value_weight,
    attn_weight,
    out_weight,
    slot_point,
    slot_rows,
    slot_bilinear,
    slot_count,
):
    owners = lax.axis_size(("tile", "query"))
    page_count = lax.axis_size("dp")
    local_queries = queries.shape[1]
    all_queries = local_queries * owners
    grad_scale = float(page_count * all_queries) ** (-0.5)
    width = features.shape[2]
    att_width = attn_weight.shape[1]
    per_head = att_width // HEADS
    head_width = width // HEADS
    exponent = jnp.exp(
        jnp.dot(queries[0], attn_weight, preferred_element_type=jnp.float32)
    ).reshape(local_queries, HEADS, per_head)
    attention = (exponent / jnp.sum(exponent, axis=2, keepdims=True)).reshape(
        local_queries, att_width
    )
    attn_rounded = attention.astype(jnp.bfloat16)
    sample_grad = times_transpose(out_grad[0], out_weight).astype(jnp.bfloat16)
    every_grad, every_attn = (
        lax.all_gather(sample_grad, ("tile", "query"), axis=0, tiled=True),
        lax.all_gather(attn_rounded, ("tile", "query"), axis=0, tiled=True),
    )
    projected = jnp.dot(features[0], value_weight, preferred_element_type=jnp.float32).astype(
        jnp.bfloat16
    )
    token_count = projected.shape[0]
    capacity = slot_point.shape[1]
    points = slot_point[0]
    alive_slot = jnp.arange(capacity, dtype=jnp.int32) < slot_count[0, 0]
    query_index = points // att_width
    attn_column = points % att_width
    head_index = attn_column // per_head
    query_match = query_index[:, None] == jnp.arange(all_queries, dtype=jnp.int32)[None, :]
    query_onehot = query_match.astype(jnp.bfloat16)
    column_match = attn_column[:, None] == jnp.arange(att_width, dtype=jnp.int32)[None, :]
    attn_rows = jnp.dot(query_onehot, every_attn, preferred_element_type=jnp.float32)
    picked_attn = jnp.sum(jnp.where(column_match, attn_rows, jnp.zeros((), jnp.float32)), axis=1)
    weight = jnp.where(alive_slot, picked_attn, jnp.zeros((), jnp.float32))
    head_mask = jnp.arange(width, dtype=jnp.int32)[None, :] // head_width == head_index[:, None]
    grad_rows = jnp.dot(query_onehot, every_grad, preferred_element_type=jnp.float32)
    slot_grad = jnp.where(head_mask, grad_rows, jnp.zeros((), jnp.float32))
    offsets = (0, 1, TILE_W, TILE_W + 1)
    padded = jnp.concatenate([projected, jnp.zeros((TILE_W + 1, width), jnp.bfloat16)], axis=0)
    corner_table = jnp.concatenate(
        [padded[offset : offset + token_count] for offset in offsets], axis=1
    )
    base_row = slot_rows[0, 0]
    picked_all = corner_table[base_row].astype(jnp.float32)
    mixed_rows = jnp.zeros((capacity, width), jnp.float32)
    corner_dots = jnp.zeros((capacity,), jnp.float32)
    contributions = []
    for corner in range(4):
        bilinear = slot_bilinear[0, corner]
        picked = picked_all[:, corner * width : (corner + 1) * width]
        mixed_rows = mixed_rows + bilinear[:, None] * picked
        corner_dots = corner_dots + bilinear * jnp.sum(picked * slot_grad, axis=1)
        contributions.append((weight * bilinear)[:, None] * slot_grad)
    corner_sums = (
        jnp.zeros((token_count, 4 * width), jnp.float32)
        .at[base_row]
        .add(jnp.concatenate(contributions, axis=1))
    )
    value_grad = corner_sums[:, 0:width]
    for corner in range(1, 4):
        value_grad = value_grad + shift_down(
            corner_sums[:, corner * width : (corner + 1) * width], offsets[corner]
        )
    query_float = query_match.astype(jnp.float32)
    sampled_part = over_rows_exact(
        query_float, jnp.where(head_mask, weight[:, None] * mixed_rows, jnp.zeros((), jnp.float32))
    )
    dots_table = jnp.where(
        jnp.logical_and(column_match, alive_slot[:, None]),
        corner_dots[:, None],
        jnp.zeros((), jnp.float32),
    )
    attn_part = over_rows_exact(query_float, dots_table)
    sampled_share, attn_grad = (
        lax.psum_scatter(sampled_part, ("tile", "query"), scatter_dimension=0, tiled=True),
        lax.psum_scatter(attn_part, ("tile", "query"), scatter_dimension=0, tiled=True),
    )
    out_term = over_rows_exact(sampled_share, out_grad[0].astype(jnp.float32))
    attn_three = attention.reshape(local_queries, HEADS, per_head)
    grad_three = attn_grad.reshape(local_queries, HEADS, per_head)
    logit_grad = (
        (attn_three * (grad_three - jnp.sum(attn_three * grad_three, axis=2, keepdims=True)))
        .reshape(local_queries, att_width)
        .astype(jnp.bfloat16)
    )
    query_grad = times_transpose(logit_grad, attn_weight).astype(jnp.bfloat16)
    value_rounded = value_grad.astype(jnp.bfloat16)
    feature_grad = times_transpose(value_rounded, value_weight).astype(jnp.bfloat16)
    value_term = over_rows(features[0], value_rounded)
    attn_term = over_rows(queries[0], logit_grad)
    summed = lax.psum((value_term, attn_term, out_term), ("tile", "query", "dp"))
    return (
        feature_grad[None],
        query_grad[None],
        summed[0] * grad_scale,
        summed[1] * grad_scale,
        summed[2] * grad_scale,
    )


def solution(mesh):
    in_specs = (
        P("dp", ("tile", "query"), None),
        P("dp", ("tile", "query"), None),
        P("dp", ("tile", "query"), None),
        P(),
        P(),
        P(),
        P("dp", ("tile", "query")),
        P("dp", None, ("tile", "query")),
        P("dp", None, ("tile", "query")),
        P("dp", ("tile", "query")),
    )
    out_specs = (P("dp", ("tile", "query"), None), P("dp", ("tile", "query"), None), P(), P(), P())
    return jax.shard_map(local, mesh=mesh, in_specs=in_specs, out_specs=out_specs, check_vma=False)
```

profile of v0, /device:TPU:1, one launch (start us, length us, event | category | flops | bytes accessed | tf_op | source)
XLA Modules:
  0.0 575.8 jit_solution(11358282747532985319)
XLA Ops:
  8.0 0.8 compare_select_fusion.2
  8.8 0.7 add_select_fusion.2
  9.5 1.0 convolution_exponential_fusion
  10.5 0.1 reshape.239
  10.6 0.1 reduce_sum.63
  10.7 0.1 div.48
  10.8 0.1 div.49
  10.9 0.9 fusion.64
  11.8 25.9 %all_gather.6 = bf16[256,128]{1,0:T(8,128)(2,1)S(1)} all-gather(bf16[8,128]{1,0:T(8,128)(2,1)S(1)} %divide_convert_fusion), channel_id=1, replica_groups=mesh['tile'=16,'query'=2,'dp'=8] {'tile','query'}, dimensions={0}, use_global_device_ids=true | all-gather | bytes 67584 | tf_op jit(solution)/shard_map/all_gather | solution.py:69
  37.7 1.1 convolution_convert_fusion.3
  38.8 24.1 %all_gather.7 = bf16[256,256]{1,0:T(8,128)(2,1)S(1)} all-gather(bf16[8,256]{1,0:T(8,128)(2,1)S(1)} %convolution_convert_fusion.3), channel_id=1, replica_groups=mesh['tile'=16,'query'=2,'dp'=8] {'tile','query'}, dimensions={0}, use_global_device_ids=true | all-gather | bytes 135168 | tf_op jit(solution)/shard_map/all_gather | solution.py:68
  62.8 1.6 convolution_convert_fusion
  64.4 1.3 pad_slice_fusion.2
  65.8 3.9 pad_maximum_fusion.1
  69.7 15.5 %gather_fusion = bf16[2048,1024]{1,0:T(8,128)(2,1)} fusion(bf16[4096,1024]{1,0:T(8,128)(2,1)} %pad_maximum_fusion.1, s32[2048]{0:T(1024)S(1)} %broadcast_clamp_fusion), kind=kCustom, calls=%fused_computation | custom fusion | bytes 8396800 | tf_op jit(solution)/shard_map/gather | solution.py:96
  85.2 6.5 %copy.27 = bf16[2048,1024]{0,1:T(8,128)(2,1)} copy(bf16[2048,1024]{1,0:T(8,128)(2,1)} %gather_fusion) | data formatting | bytes 8388608 | tf_op jit(solution)/shard_map/gather | solution.py:96
  91.7 3.3 convert_element_type.32
  94.9 0.7 fusion.27
  95.6 4.6 multiply_reduce_fusion.3
  100.3 0.5 copy-done.1
  100.7 2.4 fusion.25
  103.2 5.5 fusion.7
  108.7 0.2 all-reduce.11.cloned.1.call-start
  109.0 6.0 %pad_maximum_fusion = f32[2048,1024]{0,1:T(8,128)} fusion(f32[2048,256]{0,1:T(8,128)} %get-tuple-element.29, f32[2048,256]{0,1:T(8,128)} %get-tuple-element.30, f32[2048,256]{0,1:T(8,128)} %get-tuple-element.31, f32[2048,256]{0,1:T(8,128)} %get-tuple-element.32), kind=kLoop, calls=%fused_computation.3 | loop fusion | flops 6291456 | bytes 16777216 | tf_op jit(solution)/shard_map/concatenate | solution.py:109
  115.0 9.3 %copy.26 = f32[2048,1024]{1,0:T(8,128)} copy(f32[2048,1024]{0,1:T(8,128)} %pad_maximum_fusion) | data formatting | bytes 16777216 | tf_op jit(solution)/shard_map/concatenate | solution.py:109
  124.2 25.7 %scatter_custom_fusion = f32[4096,1024]{1,0:T(8,128)} fusion(s32[2048]{0:T(1024)S(1)} %bitcast.62, f32[2048,1024]{1,0:T(8,128)} %copy.26, f32[]{:T(128)} %constant.54.clone.1), kind=kCustom, calls=%fused_computation.5 | custom fusion | flops 2097152 | bytes 16777728 | tf_op jit(solution)/shard_map/scatter-add | solution.py:109
  149.9 2.4 slice.75
  152.4 2.4 slice.74
  154.8 2.5 slice.73
  157.3 4.7 fusion.6
  162.0 3.1 fusion.28
  165.1 0.6 dynamic-slice
  166.3 47.7 %all-reduce.9.cloned.1.call-done = f32[256,128]{1,0:T(8,128)} async-done(((f32[256,128]{1,0:T(8,128)}), f32[256,128]{1,0:T(8,128)}) %all-reduce.9.cloned.1.call-update) | async-done | bytes 131088
  214.0 0.7 constant_dynamic-slice_fusion
  214.7 0.1 reshape.240
  214.8 1.2 fusion
  216.0 0.1 sub.31
  216.1 1.6 convolution_bitcast_fusion
  217.7 83.4 %reduce-scatter.2.cloned.1.call-done = f32[8,256]{1,0:T(8,128)} async-done(((f32[256,256]{1,0:T(8,128)}), f32[8,256]{1,0:T(8,128)}) %reduce-scatter.2.cloned.1.call-update) | async-done | bytes 8208 | tf_op jit(solution)/shard_map/reduce_scatter | solution.py:127
  301.0 1.7 fusion.56
  302.8 3.7 fusion.3
  306.5 1.4 fusion.31
  307.9 256.9 %all-reduce.11.cloned.1.call-done = (f32[256,256]{0,1:T(8,128)}, f32[256,128]{0,1:T(8,128)}, f32[256,256]{0,1:T(8,128)}) async-done(((f32[256,256]{0,1:T(8,128)}, f32[256,128]{0,1:T(8,128)}, f32[256,256]{0,1:T(8,128)}), (f32[256,256]{0,1:T(8,128)}, f32[256,128]{0,1:T(8,128)}, f32[256,256]{0,1:T(8,128)})) %all-reduce.11.cloned.1.call-update) | async-done | bytes 655376 | tf_op jit(solution)/shard_map/psum | solution.py:143
  564.8 1.1 broadcast_multiply_fusion.4
  565.9 0.8 copy.31
  566.7 0.9 broadcast_multiply_fusion.6
  567.6 0.8 copy.30
  568.4 0.8 copy.29
  (25 shorter events, 0.2 us)
Async XLA Ops:
  7.2 55.7 %copy-start = (bf16[1,4096,256]{2,1,0:T(8,128)(2,1)S(1)}, bf16[1,4096,256]{2,1,0:T(8,128)(2,1)}, u32[]{:S(2)}) copy-start(bf16[1,4096,256]{2,1,0:T(8,128)(2,1)} %param.10) | copy-start | bytes 6291460
  7.2 206.8 %all-reduce.9.cloned.1.call-start = ((), (), s32[]{:S(2)}) async-start(), calls=%async_computation.2 | async-start | bytes 262144
  94.9 5.8 %copy-start.1 = (f32[2048,1024]{0,1:T(8,128)}, f32[2048,1024]{0,1:T(8,128)S(1)}, u32[]{:S(2)}) copy-start(f32[2048,1024]{0,1:T(8,128)S(1)} %convert_element_type.32) | copy-start | bytes 25165828
  103.2 197.9 %reduce-scatter.2.cloned.1.call-start = ((), (), s32[]{:S(2)}) async-start(), calls=%async_computation.1 | async-start | bytes 270336 | tf_op jit(solution)/shard_map/reduce_scatter | solution.py:127
  108.7 456.1 %all-reduce.11.cloned.1.call-start = ((), (), s32[]{:S(2)}) async-start(), calls=%async_computation.3 | async-start | bytes 1310720 | tf_op jit(solution)/shard_map/psum | solution.py:143
  162.0 3.1 copy-start.6
  162.0 54.1 %copy-start.5 = (bf16[1,8,256]{2,1,0:T(8,128)(2,1)S(1)}, bf16[1,8,256]{2,1,0:T(8,128)(2,1)}, u32[]{:S(2)}) copy-start(bf16[1,8,256]{2,1,0:T(8,128)(2,1)} %param.11) | copy-start | bytes 12292
  162.0 139.1 %copy-start.4 = (bf16[1,8,256]{2,1,0:T(8,128)(2,1)S(1)}, bf16[1,8,256]{2,1,0:T(8,128)(2,1)}, u32[]{:S(2)}) copy-start(bf16[1,8,256]{2,1,0:T(8,128)(2,1)} %param.12) | copy-start | bytes 12292
  162.0 140.8 %copy-start.2 = (bf16[256,256]{1,0:T(8,128)(2,1)S(1)}, bf16[256,256]{1,0:T(8,128)(2,1)}, u32[]{:S(2)}) copy-start(bf16[256,256]{1,0:T(8,128)(2,1)} %param.13) | copy-start | bytes 393220
  302.8 3.7 copy-start.3
Sparse Core Ops, SparseCore 0:
  103.3 110.7 all-reduce.8
  218.3 82.6 reduce-scatter.1
  307.6 257.1 all-reduce.10
where the time goes:
time: 577 us; the launch traced here: 576 us
  waiting for transfers between devices  388 us (67%)
  blocking collectives  49.9 us (9%)
  other arithmetic  48.4 us (8%)
  local copies, waits for them, and re-layouts  45.4 us (8%)
  matrix products  28.4 us (5%)
  between operations  15.3 us (3%)
    psum x1, waiting for transfers between devices, local(): lax.psum((value_term, attn_term, out_term), ('tile', 'query', 'dp'))  257 us
    reduce_scatter x1, waiting for transfers between devices, local(): lax.psum_scatter(sampled_part, ('tile', 'query'), scatter_dimension=0, ti...  83.4 us
    unnamed x4, waiting for transfers between devices  47.8 us
    all_gather x1, blocking collectives, local(): lax.all_gather(attn_rounded, ('tile', 'query'), axis=0, tiled=True)  25.9 us
    scatter-add x1, other arithmetic, local(): corner_sums = jnp.zeros((token_count, 4 * width), jnp.float32).at[base_ro...  25.7 us
    all_gather x1, blocking collectives, local(): lax.all_gather(sample_grad, ('tile', 'query'), axis=0, tiled=True)  24.1 us
    gather x2, local copies, waits for them, and re-layouts, local(): picked_all = corner_table[base_row].astype(jnp.float32)  22 us
  transfers between devices with their start and end apart: 3, of which 3 were waited for; matrix products, arithmetic and copies ran while one was open for 12% of the time, Pallas kernels for 0%

commit v1 on v0

--- a/solution.py
+++ b/solution.py
@@ -66,7 +66,15 @@
     sample_grad = times_transpose(out_grad[0], out_weight).astype(jnp.bfloat16)
     every_grad, every_attn = (
         lax.all_gather(sample_grad, ("tile", "query"), axis=0, tiled=True),
-        lax.all_gather(attn_rounded, ("tile", "query"), axis=0, tiled=True),
+        jnp.concatenate(
+            lax.all_to_all(
+                jnp.stack([attn_rounded] * lax.axis_size(("tile", "query"))),
+                ("tile", "query"),
+                0,
+                0,
+            ),
+            axis=0,
+        ),
     )
     projected = jnp.dot(features[0], value_weight, preferred_element_type=jnp.float32).astype(
         jnp.bfloat16

time: 577 us -> 622 us (1.078)
  waiting for transfers between devices: 388 us -> 442 us
  blocking collectives: 49.9 us -> 25.3 us
  starting transfers between devices: 0.3 us -> 8.7 us
  local copies, waits for them, and re-layouts: 45.4 us -> 52.8 us
    unnamed x4, waiting for transfers between devices: 47.8 us -> 102 us
    all_gather x1 -> x0, blocking collectives: 25.9 us -> none  [local(): lax.all_gather(attn_rounded, ('tile', 'query'), axis=0, tiled=True)]
    all_to_all x0 -> x1, starting transfers between devices: none -> 8.58 us  [local(): lax.all_to_all(jnp.stack([attn_rounded] * lax.axis_size(('tile', 'query')...]
  transfers between devices with their start and end apart: 3 -> 4, of which waited for: 3 -> 3; matrix products, arithmetic and copies ran while one was open for 12% -> 9% of each run, Pallas kernels for 0% -> 0%
where the time goes in v1:
time: 622 us; the launch traced here: 621 us
  waiting for transfers between devices  442 us (71%)
  local copies, waits for them, and re-layouts  52.8 us (8%)
  other arithmetic  51.8 us (8%)
  matrix products  25.6 us (4%)
  blocking collectives  25.3 us (4%)
  between operations  15.2 us (2%)
  starting transfers between devices  8.7 us (1%)
    psum x1, waiting for transfers between devices, local(): lax.psum((value_term, attn_term, out_term), ('tile', 'query', 'dp'))  257 us
    unnamed x4, waiting for transfers between devices  102 us
    reduce_scatter x1, waiting for transfers between devices, local(): lax.psum_scatter(sampled_part, ('tile', 'query'), scatter_dimension=0, ti...  83.4 us
    scatter-add x1, other arithmetic, local(): corner_sums = jnp.zeros((token_count, 4 * width), jnp.float32).at[base_ro...  25.7 us
    all_gather x1, blocking collectives, local(): lax.all_gather(sample_grad, ('tile', 'query'), axis=0, tiled=True)  25.3 us
    gather x2, local copies, waits for them, and re-layouts, local(): picked_all = corner_table[base_row].astype(jnp.float32)  22 us
    slice x3, local copies, waits for them, and re-layouts, shift_down(): block[:block.shape[0] - offset]  13.2 us
  transfers between devices with their start and end apart: 4, of which 3 were waited for; matrix products, arithmetic and copies ran while one was open for 9% of the time, Pallas kernels for 0%

profile of v1, /device:TPU:1, one launch (start us, length us, event | category | flops | bytes accessed | tf_op | source)
XLA Modules:
  0.0 621.3 jit_solution(14760448857361540239)
XLA Ops:
  7.2 1.1 convolution_exponential_fusion
  8.3 0.1 reshape.244
  8.4 0.1 reduce_sum.63
  8.5 0.1 div.48
  8.6 0.1 div.49
  8.7 0.6 stack.2
  9.3 8.6 %all-to-all-start = ((bf16[32,8,128]{2,1,0:T(8,128)(2,1)}), bf16[32,8,128]{2,1,0:T(8,128)(2,1)S(1)}, u32[]{:S(2)}, u32[]{:S(2)}) async-start(bf16[32,8,128]{2,1,0:T(8,128)(2,1)} %stack.2), calls=%async_computation | async-start | bytes 131072 | tf_op jit(solution)/shard_map/all_to_all | solution.py:70
  18.6 0.8 compare_select_fusion.2
  19.4 0.7 add_select_fusion.2
  20.1 0.9 fusion.65
  21.1 1.6 convolution_convert_fusion
  22.7 1.3 pad_slice_fusion.2
  24.0 0.1 convolution_convert_fusion.3
  24.2 3.9 pad_maximum_fusion.1
  28.1 15.5 %gather_fusion = bf16[2048,1024]{1,0:T(8,128)(2,1)} fusion(bf16[4096,1024]{1,0:T(8,128)(2,1)} %pad_maximum_fusion.1, s32[2048]{0:T(1024)S(1)} %broadcast_clamp_fusion), kind=kCustom, calls=%fused_computation | custom fusion | bytes 8396800 | tf_op jit(solution)/shard_map/gather | solution.py:104
  43.6 6.5 %copy.27 = bf16[2048,1024]{0,1:T(8,128)(2,1)} copy(bf16[2048,1024]{1,0:T(8,128)(2,1)} %gather_fusion) | data formatting | bytes 8388608 | tf_op jit(solution)/shard_map/gather | solution.py:104
  50.1 6.5 %convert_element_type.32 = f32[2048,1024]{0,1:T(8,128)} convert(bf16[2048,1024]{0,1:T(8,128)(2,1)} %copy.27) | non-fusion elementwise | flops 2097152 | bytes 12582912 | tf_op jit(solution)/shard_map/convert_element_type | solution.py:104
  56.6 0.6 dynamic-slice
  57.8 25.3 %all_gather.3 = bf16[256,256]{1,0:T(8,128)(2,1)S(1)} all-gather(bf16[8,256]{1,0:T(8,128)(2,1)S(1)} %convolution_convert_fusion.3), channel_id=1, replica_groups=mesh['tile'=16,'query'=2,'dp'=8] {'tile','query'}, dimensions={0}, use_global_device_ids=true | all-gather | bytes 135168 | tf_op jit(solution)/shard_map/all_gather | solution.py:68
  83.1 0.7 fusion.27
  83.8 5.5 fusion.7
  89.3 4.3 multiply_reduce_fusion.3
  93.7 3.8 pad_maximum_fusion
  97.5 9.3 %copy.26 = f32[2048,1024]{1,0:T(8,128)} copy(f32[2048,1024]{0,1:T(8,128)} %pad_maximum_fusion) | data formatting | bytes 16777216 | tf_op jit(solution)/shard_map/concatenate | solution.py:117
  106.8 25.7 %scatter_custom_fusion = f32[4096,1024]{1,0:T(8,128)} fusion(s32[2048]{0:T(1024)S(1)} %bitcast.64, f32[2048,1024]{1,0:T(8,128)} %copy.26, f32[]{:T(128)} %constant.54.clone.1), kind=kCustom, calls=%fused_computation.5 | custom fusion | flops 2097152 | bytes 16777728 | tf_op jit(solution)/shard_map/scatter-add | solution.py:117
  132.5 4.4 slice.75
  136.9 4.4 slice.74
  141.3 4.4 slice.73
  145.6 2.4 fusion.25
  148.1 7.0 %fusion.6 = bf16[4096,256]{1,0:T(8,128)(2,1)S(1)} fusion(f32[4096,1024]{1,0:T(8,128)} %scatter_custom_fusion, f32[4031,256]{1,0:T(8,128)} %slice.75, f32[4032,256]{1,0:T(8,128)} %slice.74, f32[4095,256]{1,0:T(8,128)} %slice.73), kind=kLoop, calls=%fused_computation.13 | loop fusion | flops 4194304 | bytes 18741248 | tf_op jit(solution)/shard_map/convert_element_type | solution.py:147
  155.1 1.3 copy-done.1
  156.4 1.4 fusion.28
  158.0 101.6 %all-reduce.9.cloned.1.call-done = f32[256,128]{1,0:T(8,128)} async-done(((f32[256,128]{1,0:T(8,128)}), f32[256,128]{1,0:T(8,128)}) %all-reduce.9.cloned.1.call-update) | async-done | bytes 131088
  259.5 0.7 constant_dynamic-slice_fusion
  260.2 0.1 reshape.246
  260.3 1.2 fusion
  261.5 0.1 sub.31
  261.6 1.6 convolution_bitcast_fusion
  263.2 83.4 %reduce-scatter.2.cloned.1.call-done = f32[8,256]{1,0:T(8,128)} async-done(((f32[256,256]{1,0:T(8,128)}), f32[8,256]{1,0:T(8,128)}) %reduce-scatter.2.cloned.1.call-update) | async-done | bytes 8208 | tf_op jit(solution)/shard_map/reduce_scatter | solution.py:135
  346.6 1.7 fusion.57
  348.3 3.7 fusion.3
  352.0 1.4 fusion.31
  353.4 256.9 %all-reduce.11.cloned.1.call-done = (f32[256,256]{0,1:T(8,128)}, f32[256,128]{0,1:T(8,128)}, f32[256,256]{0,1:T(8,128)}) async-done(((f32[256,256]{0,1:T(8,128)}, f32[256,128]{0,1:T(8,128)}, f32[256,256]{0,1:T(8,128)}), (f32[256,256]{0,1:T(8,128)}, f32[256,128]{0,1:T(8,128)}, f32[256,256]{0,1:T(8,128)})) %all-reduce.11.cloned.1.call-update) | async-done | bytes 655376 | tf_op jit(solution)/shard_map/psum | solution.py:151
  610.3 1.1 broadcast_multiply_fusion.4
  611.4 0.8 copy.31
  612.2 0.9 broadcast_multiply_fusion.6
  613.1 0.8 copy.30
  613.9 0.8 copy.29
  (29 shorter events, 0.3 us)
Async XLA Ops:
  7.2 13.9 %copy-start = (bf16[1,4096,256]{2,1,0:T(8,128)(2,1)S(1)}, bf16[1,4096,256]{2,1,0:T(8,128)(2,1)}, u32[]{:S(2)}) copy-start(bf16[1,4096,256]{2,1,0:T(8,128)(2,1)} %param.10) | copy-start | bytes 6291460
  9.3 73.8 %all-to-all-start = ((bf16[32,8,128]{2,1,0:T(8,128)(2,1)}), bf16[32,8,128]{2,1,0:T(8,128)(2,1)S(1)}, u32[]{:S(2)}, u32[]{:S(2)}) async-start(bf16[32,8,128]{2,1,0:T(8,128)(2,1)} %stack.2), calls=%async_computation | async-start | bytes 131072 | tf_op jit(solution)/shard_map/all_to_all | solution.py:70
  17.9 241.7 %all-reduce.9.cloned.1.call-start = ((), (), s32[]{:S(2)}) async-start(), calls=%async_computation.3 | async-start | bytes 262144
  22.7 1.3 copy-start.4
  22.7 1.3 copy-start.5
  50.1 6.5 %copy-start.7 = (u32[256]{0:T(256)S(1)}, u32[256]{0:T(256)}, u32[]{:S(2)}) copy-start(u32[256]{0:T(256)} %constant.85) | copy-start | bytes 3076
  148.1 198.5 %reduce-scatter.2.cloned.1.call-start = ((), (), s32[]{:S(2)}) async-start(), calls=%async_computation.2 | async-start | bytes 270336 | tf_op jit(solution)/shard_map/reduce_scatter | solution.py:135
  155.1 1.4 copy-start.1
  156.4 105.1 %copy-start.6 = (bf16[1,8,256]{2,1,0:T(8,128)(2,1)S(1)}, bf16[1,8,256]{2,1,0:T(8,128)(2,1)}, u32[]{:S(2)}) copy-start(bf16[1,8,256]{2,1,0:T(8,128)(2,1)} %param.11) | copy-start | bytes 12292
  156.4 191.9 %copy-start.2 = (bf16[256,256]{1,0:T(8,128)(2,1)S(1)}, bf16[256,256]{1,0:T(8,128)(2,1)}, u32[]{:S(2)}) copy-start(bf16[256,256]{1,0:T(8,128)(2,1)} %param.13) | copy-start | bytes 393220
  157.9 452.4 %all-reduce.11.cloned.1.call-start = ((), (), s32[]{:S(2)}) async-start(), calls=%async_computation.4 | async-start | bytes 1310720 | tf_op jit(solution)/shard_map/psum | solution.py:151
  348.3 3.7 copy-start.3
Sparse Core Ops, SparseCore 0:
  148.2 111.3 all-reduce.8
  263.8 82.6 reduce-scatter.1
  353.1 257.1 all-reduce.10
